TPU v7x, 256 devices: a whole 4x4x8 slice. The times are simulated.
256 devices in a mesh: prow: 64 (over x, z, core), pcol: 4 (over y).
Axes of the slice: x: 4, y: 4, z: 8, core: 2. Of those that a mesh axis runs over, the one named last changes fastest.
Arguments:
- right_side: float32 [512, 65536], P('pcol', 'prow'), may hold values from -6 to 6
- factor: float32 [65536, 2048], P('prow', 'pcol'), may hold values from -0.125 to 0.125
- inverses: float32 [2048, 512], replicated, as said below
Outputs:
- solved: float32 [512, 65536], P('pcol', 'prow')
Inputs may be any that keep to these rules, and one draw needn't show every extreme that they name: Each 512 x 512 block of inverses is lower triangular with a positive diagonal.
All inputs are finite; a program needn't handle non-finite values.
Results may differ from a plain program's by a relative error of at most 0.0001.
Values sent between devices are 32-bit elements; how exact they have to be, the bound alone decides.
No kernel may reach another device: no remote copies, remote signals or barrier semaphores. Data moves between devices by JAX's collectives and lax.ppermute only.
A program may use at most 64 MiB of HBM per device.

v0:
```python
import jax
import jax.numpy as jnp
from jax import lax
from jax.sharding import PartitionSpec as P


def spread(block, axis, source):
    block = jnp.where(lax.axis_index(axis) == source, block, jnp.zeros_like(block))
    return lax.psum(block, axis)


def contract(left, right):
    return lax.dot_general(
        left,
        right,
        (((1,), (1,)), ((), ())),
        precision=lax.Precision.HIGHEST,
        preferred_element_type=jnp.float32,
    )


def per_device(right_side, factor, inverses):
    block = factor.shape[1]
    rhs_width = right_side.shape[0]
    sections = lax.axis_size("pcol")
    all_samples = rhs_width * sections
    row_at = lax.axis_index("prow")
    col_at = lax.axis_index("pcol")
    top_block = factor[:block]
    panel_own = jnp.zeros((all_samples, block), jnp.float32)
    solved_head = jnp.zeros((rhs_width, block), jnp.float32)
    own_panels = []
    for section in range(sections):
        current = right_side[:, :block]
        if section > 0:
            current = current - lax.psum_scatter(
                contract(panel_own, top_block), "pcol", scatter_dimension=0, tiled=True
            )
        block_inverse = inverses[section * block : (section + 1) * block]
        solved_part = contract(current, block_inverse)
        solved_head = jnp.where(row_at == section, solved_part, solved_head)
        gathered = lax.all_gather(solved_part, "pcol", axis=0, tiled=True)
        panel_full = spread(gathered, "prow", section)
        panel_own = jnp.where(col_at == section, panel_full, panel_own)
        own_panels.append(lax.dynamic_slice_in_dim(panel_full, col_at * rhs_width, rhs_width, 0))
    updated = right_side - lax.psum_scatter(
        contract(panel_own, factor), "pcol", scatter_dimension=0, tiled=True
    )
    head_block = jnp.where(row_at < sections, solved_head, updated[:, :block])
    return jnp.concatenate([head_block, updated[:, block:]], axis=1)


def solution(mesh):
    return jax.shard_map(
        per_device,
        mesh=mesh,
        in_specs=(P("pcol", "prow"), P("prow", "pcol"), P()),
        out_specs=P("pcol", "prow"),
        check_vma=False,
    )
```

profile of v0, /device:TPU:1, one launch (start us, length us, event | category | flops | bytes accessed | tf_op | source)
XLA Modules:
  0.0 1011.9 jit_solution(13477425533814743867)
XLA Ops:
  6.5 3.2 fusion.8
  9.7 0.0 all-reduce.5.cloned.1.call-start
  9.8 29.5 %all-gather.5.cloned.1.call-done = f32[512,512]{1,0:T(8,128)} async-done(((f32[128,512]{1,0:T(8,128)}), f32[512,512]{1,0:T(8,128)}) %all-gather.5.cloned.1.call-update) | async-done | bytes 1048592 | tf_op jit(solution)/shard_map/all_gather | solution.py:42
  39.3 1.1 broadcast_select_fusion.3
  40.5 187.1 %all-reduce.5.cloned.1.call-done = f32[512,512]{1,0:T(8,128)} async-done(((f32[512,512]{1,0:T(8,128)}), f32[512,512]{1,0:T(8,128)}) %all-reduce.5.cloned.1.call-update) | async-done | bytes 1048592 | tf_op jit(solution)/shard_map/psum | solution.py:9
  227.6 4.1 fusion.10
  231.8 22.7 %reduce-scatter.5.cloned.1.call-done = f32[128,512]{1,0:T(8,128)} async-done(((f32[512,512]{1,0:T(8,128)}), f32[128,512]{1,0:T(8,128)}) %reduce-scatter.5.cloned.1.call-update) | async-done | bytes 262160 | tf_op jit(solution)/shard_map/reduce_scatter | solution.py:36
  254.5 3.2 fusion.6
  257.7 0.0 all-reduce.7.cloned.1.call-start
  257.8 26.9 %all-gather.7.cloned.1.call-done = f32[512,512]{1,0:T(8,128)} async-done(((f32[128,512]{1,0:T(8,128)}), f32[512,512]{1,0:T(8,128)}) %all-gather.7.cloned.1.call-update) | async-done | bytes 1048592 | tf_op jit(solution)/shard_map/all_gather | solution.py:42
  284.6 2.3 broadcast_select_fusion.2
  286.9 0.0 reduce-scatter.7.cloned.1.call-start
  287.0 185.8 %all-reduce.7.cloned.1.call-done = f32[512,512]{1,0:T(8,128)} async-done(((f32[512,512]{1,0:T(8,128)}), f32[512,512]{1,0:T(8,128)}) %all-reduce.7.cloned.1.call-update) | async-done | bytes 1048592 | tf_op jit(solution)/shard_map/psum | solution.py:9
  472.8 1.4 select_select_fusion
  474.2 2.8 fusion.14
  477.1 22.7 %reduce-scatter.7.cloned.1.call-done = f32[128,512]{1,0:T(8,128)} async-done(((f32[512,512]{1,0:T(8,128)}), f32[128,512]{1,0:T(8,128)}) %reduce-scatter.7.cloned.1.call-update) | async-done | bytes 262160 | tf_op jit(solution)/shard_map/reduce_scatter | solution.py:36
  499.9 3.3 fusion.4
  503.2 26.9 %all-gather.9.cloned.1.call-done = f32[512,512]{1,0:T(8,128)} async-done(((f32[128,512]{1,0:T(8,128)}), f32[512,512]{1,0:T(8,128)}) %all-gather.9.cloned.1.call-update) | async-done | bytes 1048592 | tf_op jit(solution)/shard_map/all_gather | solution.py:42
  530.2 1.1 broadcast_select_fusion.1
  531.3 187.1 %all-reduce.9.cloned.1.call-done = f32[512,512]{1,0:T(8,128)} async-done(((f32[512,512]{1,0:T(8,128)}), f32[512,512]{1,0:T(8,128)}) %all-reduce.9.cloned.1.call-update) | async-done | bytes 1048592 | tf_op jit(solution)/shard_map/psum | solution.py:9
  718.4 2.8 fusion.12
  721.4 25.3 %reduce-scatter.9.cloned.1.call-done = f32[128,512]{1,0:T(8,128)} async-done(((f32[512,512]{1,0:T(8,128)}), f32[128,512]{1,0:T(8,128)}) %reduce-scatter.9.cloned.1.call-update) | async-done | bytes 262160 | tf_op jit(solution)/shard_map/reduce_scatter | solution.py:36
  746.6 3.3 fusion.2
  750.0 26.9 %all-gather.11.cloned.1.call-done = f32[512,512]{1,0:T(8,128)} async-done(((f32[128,512]{1,0:T(8,128)}), f32[512,512]{1,0:T(8,128)}) %all-gather.11.cloned.1.call-update) | async-done | bytes 1048592 | tf_op jit(solution)/shard_map/all_gather | solution.py:42
  776.8 1.1 broadcast_select_fusion
  777.9 0.2 reduce-scatter.11.cloned.1.call-start
  778.2 186.9 %all-reduce.11.cloned.1.call-done = f32[512,512]{1,0:T(8,128)} async-done(((f32[512,512]{1,0:T(8,128)}), f32[512,512]{1,0:T(8,128)}) %all-reduce.11.cloned.1.call-update) | async-done | bytes 1048592 | tf_op jit(solution)/shard_map/psum | solution.py:9
  965.1 4.9 fusion
  970.1 32.8 %reduce-scatter.11.cloned.1.call-done = f32[128,1024]{1,0:T(8,128)} async-done(((f32[512,1024]{1,0:T(8,128)}), f32[128,1024]{1,0:T(8,128)}) %reduce-scatter.11.cloned.1.call-update) | async-done | bytes 524304 | tf_op jit(solution)/shard_map/reduce_scatter | solution.py:46
  1002.9 1.1 sub.15
  1004.1 0.2 slice_select_fusion
  1004.2 0.8 copy-done.7
  (36 shorter events, 0.5 us)
Async XLA Ops:
  6.5 32.8 %all-gather.5.cloned.1.call-start = ((), (), s32[]{:S(2)}) async-start(), calls=%async_computation.4 | async-start | bytes 1310720 | tf_op jit(solution)/shard_map/all_gather | solution.py:42
  9.7 217.9 %copy-start = (f32[1024,512]{1,0:T(8,128)S(1)}, f32[1024,512]{1,0:T(8,128)}, u32[]{:S(2)}) copy-start(f32[1024,512]{1,0:T(8,128)} %param.4) | copy-start | bytes 6291460
  9.7 217.9 %all-reduce.5.cloned.1.call-start = ((), (), s32[]{:S(2)}) async-start(), calls=%async_computation.5 | async-start | bytes 2097152 | tf_op jit(solution)/shard_map/psum | solution.py:9
  40.4 214.1 %reduce-scatter.5.cloned.1.call-start = ((), (), s32[]{:S(2)}) async-start(), calls=%async_computation.6 | async-start | bytes 1310720 | tf_op jit(solution)/shard_map/reduce_scatter | solution.py:36
  40.5 214.0 %copy-start.1 = (f32[128,1024]{1,0:T(8,128)S(1)}, f32[128,1024]{1,0:T(8,128)}, u32[]{:S(2)}) copy-start(f32[128,1024]{1,0:T(8,128)} %param.3) | copy-start | bytes 1572868
  231.7 52.9 %all-gather.7.cloned.1.call-start = ((), (), s32[]{:S(2)}) async-start(), calls=%async_computation.7 | async-start | bytes 1310720 | tf_op jit(solution)/shard_map/all_gather | solution.py:42
  257.7 215.0 %all-reduce.7.cloned.1.call-start = ((), (), s32[]{:S(2)}) async-start(), calls=%async_computation.8 | async-start | bytes 2097152 | tf_op jit(solution)/shard_map/psum | solution.py:9
  286.9 212.9 %reduce-scatter.7.cloned.1.call-start = ((), (), s32[]{:S(2)}) async-start(), calls=%async_computation.9 | async-start | bytes 1310720 | tf_op jit(solution)/shard_map/reduce_scatter | solution.py:36
  477.1 53.1 %all-gather.9.cloned.1.call-start = ((), (), s32[]{:S(2)}) async-start(), calls=%async_computation.10 | async-start | bytes 1310720 | tf_op jit(solution)/shard_map/all_gather | solution.py:42
  503.2 215.3 %all-reduce.9.cloned.1.call-start = ((), (), s32[]{:S(2)}) async-start(), calls=%async_computation.11 | async-start | bytes 2097152 | tf_op jit(solution)/shard_map/psum | solution.py:9
  531.3 215.3 %reduce-scatter.9.cloned.1.call-start = ((), (), s32[]{:S(2)}) async-start(), calls=%async_computation.12 | async-start | bytes 1310720 | tf_op jit(solution)/shard_map/reduce_scatter | solution.py:36
  721.3 55.5 %all-gather.11.cloned.1.call-start = ((), (), s32[]{:S(2)}) async-start(), calls=%async_computation.13 | async-start | bytes 1310720 | tf_op jit(solution)/shard_map/all_gather | solution.py:42
  749.9 215.2 %all-reduce.11.cloned.1.call-start = ((), (), s32[]{:S(2)}) async-start(), calls=%async_computation.14 | async-start | bytes 2097152 | tf_op jit(solution)/shard_map/psum | solution.py:9
  777.9 225.0 %reduce-scatter.11.cloned.1.call-start = ((), (), s32[]{:S(2)}) async-start(), calls=%async_computation.15 | async-start | bytes 2621440 | tf_op jit(solution)/shard_map/reduce_scatter | solution.py:46
  970.0 32.9 %copy-start.2 = (f32[128,1024]{1,0:T(8,128)S(1)}, f32[128,1024]{1,0:T(8,128)}, u32[]{:S(2)}) copy-start(f32[128,1024]{1,0:T(8,128)} %param.3) | copy-start | bytes 1572868
  970.0 34.0 %copy-start.3 = (f32[128,512]{1,0:T(8,128)S(1)}, f32[128,512]{1,0:T(8,128)}, u32[]{:S(2)}) copy-start(f32[128,512]{1,0:T(8,128)} %fusion.6) | copy-start | bytes 786436
  970.0 34.0 %copy-start.4 = (f32[128,512]{1,0:T(8,128)S(1)}, f32[128,512]{1,0:T(8,128)}, u32[]{:S(2)}) copy-start(f32[128,512]{1,0:T(8,128)} %fusion.4) | copy-start | bytes 786436
  970.0 34.0 %copy-start.5 = (f32[128,512]{1,0:T(8,128)S(1)}, f32[128,512]{1,0:T(8,128)}, u32[]{:S(2)}) copy-start(f32[128,512]{1,0:T(8,128)} %fusion.2) | copy-start | bytes 786436
  970.0 34.0 %copy-start.6 = (f32[128,512]{1,0:T(8,128)S(1)}, f32[128,512]{1,0:T(8,128)}, u32[]{:S(2)}) copy-start(f32[128,512]{1,0:T(8,128)} %fusion.8) | copy-start | bytes 786436
  1004.2 0.8 copy-start.7
Sparse Core Ops, SparseCore 0:
  9.9 29.4 all-gather.4
  42.8 184.8 all-reduce.4
  231.8 22.6 reduce-scatter.4
  257.8 26.7 all-gather.6
  287.9 184.8 all-reduce.6
  477.2 22.6 reduce-scatter.6
  503.3 26.8 all-gather.8
  533.6 184.8 all-reduce.8
  721.4 25.1 reduce-scatter.8
  750.0 26.7 all-gather.10
  780.3 184.8 all-reduce.10
  970.2 32.6 reduce-scatter.10
where the time goes:
time: 1010 us
  waiting for transfers between devices  961 us (95%)
  matrix products  27.6 us (3%)
  between operations  13.7 us (1%)
    psum x4, waiting for transfers between devices, spread(): return lax.psum(block, axis)  747 us
    all_gather x4, waiting for transfers between devices, per_device(): gathered = lax.all_gather(solved_part, 'pcol', axis=0, tiled=True)  110 us
    reduce_scatter x3, waiting for transfers between devices, per_device(): lax.psum_scatter(contract(panel_own, top_block), 'pcol', scatter_dimensio...  70.7 us
    reduce_scatter x1, waiting for transfers between devices, per_device(): lax.psum_scatter(contract(panel_own, factor), 'pcol', scatter_dimension=0...  32.8 us
    dot_general x8, matrix products, contract(): lax.dot_general(left, right, (((1,), (1,)), ((), ())), precision=lax.Prec...  27.6 us
  transfers between devices with their start and end apart: 12, of which 12 were waited for; matrix products, arithmetic and copies ran while one was open for 0% of the time, Pallas kernels for 0%

commit v1 on v0

--- a/solution.py
+++ b/solution.py
@@ -2,6 +2,19 @@
 import jax.numpy as jnp
 from jax import lax
 from jax.sharding import PartitionSpec as P
+
+
+def ring_gather(x, axis, dim):
+    ways = lax.axis_size(axis)
+    up = [(d, (d + 1) % ways) for d in range(ways)]
+    down = [(d, (d - 1) % ways) for d in range(ways)]
+    earlier, later = ([x], [x])
+    for _ in range(ways // 2):
+        earlier.append(lax.ppermute(earlier[-1], axis, up))
+    for _ in range((ways - 1) // 2):
+        later.append(lax.ppermute(later[-1], axis, down))
+    line = jnp.concatenate([*earlier[::-1], *later[1:]], axis=dim)
+    return jnp.roll(line, (lax.axis_index(axis) - ways // 2) * x.shape[dim], axis=dim)
 
 
 def spread(block, axis, source):
@@ -39,7 +52,7 @@
         block_inverse = inverses[section * block : (section + 1) * block]
         solved_part = contract(current, block_inverse)
         solved_head = jnp.where(row_at == section, solved_part, solved_head)
-        gathered = lax.all_gather(solved_part, "pcol", axis=0, tiled=True)
+        gathered = ring_gather(solved_part, "pcol", 0)
         panel_full = spread(gathered, "prow", section)
         panel_own = jnp.where(col_at == section, panel_full, panel_own)
         own_panels.append(lax.dynamic_slice_in_dim(panel_full, col_at * rhs_width, rhs_width, 0))

time: 1010 us -> 962 us (0.952)
  waiting for transfers between devices: 961 us -> 893 us
  starting transfers between devices: 0.64 us -> 14.1 us
    all_gather x4 -> x0, waiting for transfers between devices: 110 us -> none  [per_device(): gathered = lax.all_gather(solved_part, 'pcol', axis=0, tiled=True)]
    ppermute x0 -> x12, waiting for transfers between devices: none -> 42.5 us  [the longest x8 42.5 us: ring_gather(): earlier.append(lax.ppermute(earlier[-1], axis, up))]
    ppermute x0 -> x12, starting transfers between devices: none -> 13.6 us  [the longest x4 9.54 us: ring_gather(): later.append(lax.ppermute(later[-1], axis, down))]
  transfers between devices with their start and end apart: 12 -> 20, of which waited for: 12 -> 16; matrix products, arithmetic and copies ran while one was open for 0% -> 0% of each run, Pallas kernels for 0% -> 0%
where the time goes in v1:
time: 962 us
  waiting for transfers between devices  893 us (93%)
  matrix products  26.3 us (3%)
  other arithmetic  14.4 us (1%)
  starting transfers between devices  14.1 us (1%)
  between operations  13.6 us (1%)
    psum x4, waiting for transfers between devices, spread(): return lax.psum(block, axis)  746 us
    reduce_scatter x3, waiting for transfers between devices, per_device(): lax.psum_scatter(contract(panel_own, top_block), 'pcol', scatter_dimensio...  70.8 us
    ppermute x8, waiting for transfers between devices, ring_gather(): earlier.append(lax.ppermute(earlier[-1], axis, up))  42.5 us
    reduce_scatter x1, waiting for transfers between devices, per_device(): lax.psum_scatter(contract(panel_own, factor), 'pcol', scatter_dimension=0...  32.8 us
    dot_general x8, matrix products, contract(): lax.dot_general(left, right, (((1,), (1,)), ((), ())), precision=lax.Prec...  26.3 us
  transfers between devices with their start and end apart: 20, of which 16 were waited for; matrix products, arithmetic and copies ran while one was open for 0% of the time, Pallas kernels for 0%

profile of v1, /device:TPU:1, one launch (start us, length us, event | category | flops | bytes accessed | tf_op | source)
XLA Modules:
  0.0 961.7 jit_solution(15465789154658361334)
XLA Ops:
  6.5 2.6 fusion.40
  9.2 2.2 collective-permute-start
  12.9 3.7 collective-permute-done
  18.4 5.4 collective-permute-done.1
  23.7 2.5 fusion.28
  26.4 188.4 %all-reduce.5.cloned.1.call-done = f32[512,512]{1,0:T(8,128)} async-done(((f32[512,512]{1,0:T(8,128)}), f32[512,512]{1,0:T(8,128)}) %all-reduce.5.cloned.1.call-update) | async-done | bytes 1048592 | tf_op jit(solution)/shard_map/psum | solution.py:22
  214.8 4.1 fusion.42
  219.0 22.7 %reduce-scatter.5.cloned.1.call-done = f32[128,512]{1,0:T(8,128)} async-done(((f32[512,512]{1,0:T(8,128)}), f32[128,512]{1,0:T(8,128)}) %reduce-scatter.5.cloned.1.call-update) | async-done | bytes 262160 | tf_op jit(solution)/shard_map/reduce_scatter | solution.py:49
  241.7 2.5 fusion.38
  244.3 2.7 collective-permute-start.5
  246.9 4.2 collective-permute-done.3
  251.2 6.4 collective-permute-done.4
  257.6 2.5 fusion.20
  260.4 186.0 %all-reduce.7.cloned.1.call-done = f32[512,512]{1,0:T(8,128)} async-done(((f32[512,512]{1,0:T(8,128)}), f32[512,512]{1,0:T(8,128)}) %all-reduce.7.cloned.1.call-update) | async-done | bytes 1048592 | tf_op jit(solution)/shard_map/psum | solution.py:22
  447.8 2.8 fusion.46
  450.7 22.8 %reduce-scatter.7.cloned.1.call-done = f32[128,512]{1,0:T(8,128)} async-done(((f32[512,512]{1,0:T(8,128)}), f32[128,512]{1,0:T(8,128)}) %reduce-scatter.7.cloned.1.call-update) | async-done | bytes 262160 | tf_op jit(solution)/shard_map/reduce_scatter | solution.py:49
  473.5 3.3 fusion.36
  476.8 2.7 collective-permute-start.8
  479.4 4.6 collective-permute-done.6
  484.1 6.7 collective-permute-done.7
  490.8 3.3 fusion.12
  494.2 186.0 %all-reduce.9.cloned.1.call-done = f32[512,512]{1,0:T(8,128)} async-done(((f32[512,512]{1,0:T(8,128)}), f32[512,512]{1,0:T(8,128)}) %all-reduce.9.cloned.1.call-update) | async-done | bytes 1048592 | tf_op jit(solution)/shard_map/psum | solution.py:22
  680.2 2.8 fusion.44
  683.1 25.3 %reduce-scatter.9.cloned.1.call-done = f32[128,512]{1,0:T(8,128)} async-done(((f32[512,512]{1,0:T(8,128)}), f32[128,512]{1,0:T(8,128)}) %reduce-scatter.9.cloned.1.call-update) | async-done | bytes 262160 | tf_op jit(solution)/shard_map/reduce_scatter | solution.py:49
  708.4 3.3 fusion.34
  711.6 2.7 collective-permute-start.11
  714.3 4.7 collective-permute-done.9
  719.0 6.7 collective-permute-done.10
  725.8 3.3 fusion.4
  729.1 185.9 %all-reduce.11.cloned.1.call-done = f32[512,512]{1,0:T(8,128)} async-done(((f32[512,512]{1,0:T(8,128)}), f32[512,512]{1,0:T(8,128)}) %all-reduce.11.cloned.1.call-update) | async-done | bytes 1048592 | tf_op jit(solution)/shard_map/psum | solution.py:22
  915.0 4.9 fusion.32
  919.9 32.8 %reduce-scatter.11.cloned.1.call-done = f32[128,1024]{1,0:T(8,128)} async-done(((f32[512,1024]{1,0:T(8,128)}), f32[128,1024]{1,0:T(8,128)}) %reduce-scatter.11.cloned.1.call-update) | async-done | bytes 524304 | tf_op jit(solution)/shard_map/reduce_scatter | solution.py:59
  (44 shorter events, 7.6 us)
Async XLA Ops:
  6.5 208.3 %copy-start = (f32[1024,512]{1,0:T(8,128)S(1)}, f32[1024,512]{1,0:T(8,128)}, u32[]{:S(2)}) copy-start(f32[1024,512]{1,0:T(8,128)} %param.6) | copy-start | bytes 6291460
  6.5 208.3 %all-reduce.5.cloned.1.call-start = ((), (), s32[]{:S(2)}) async-start(), calls=%async_computation.4 | async-start | bytes 2097152 | tf_op jit(solution)/shard_map/psum | solution.py:22
  9.2 17.2 %copy-start.3 = (f32[128,512]{1,0:T(8,128)}, f32[128,512]{1,0:T(8,128)S(1)}, u32[]{:S(2)}) copy-start(f32[128,512]{1,0:T(8,128)S(1)} %fusion.40) | copy-start | bytes 786436
  9.2 7.4 collective-permute-start
  11.4 7.0 collective-permute-start.2
  16.6 7.2 collective-permute-start.1
  26.3 215.4 %reduce-scatter.5.cloned.1.call-start = ((), (), s32[]{:S(2)}) async-start(), calls=%async_computation.5 | async-start | bytes 1310720 | tf_op jit(solution)/shard_map/reduce_scatter | solution.py:49
  26.4 215.3 %copy-start.1 = (f32[128,1024]{1,0:T(8,128)S(1)}, f32[128,1024]{1,0:T(8,128)}, u32[]{:S(2)}) copy-start(f32[128,1024]{1,0:T(8,128)} %param.5) | copy-start | bytes 1572868
  218.9 227.5 %all-reduce.7.cloned.1.call-start = ((), (), s32[]{:S(2)}) async-start(), calls=%async_computation.6 | async-start | bytes 2097152 | tf_op jit(solution)/shard_map/psum | solution.py:22
  244.2 7.0 collective-permute-start.3
  244.3 6.9 collective-permute-start.5
  251.2 6.4 collective-permute-start.4
  260.2 213.3 %reduce-scatter.7.cloned.1.call-start = ((), (), s32[]{:S(2)}) async-start(), calls=%async_computation.7 | async-start | bytes 1310720 | tf_op jit(solution)/shard_map/reduce_scatter | solution.py:49
  450.7 229.5 %all-reduce.9.cloned.1.call-start = ((), (), s32[]{:S(2)}) async-start(), calls=%async_computation.8 | async-start | bytes 2097152 | tf_op jit(solution)/shard_map/psum | solution.py:22
  476.8 7.3 collective-permute-start.6
  476.8 7.3 collective-permute-start.8
  484.1 6.7 collective-permute-start.7
  494.1 214.2 %reduce-scatter.9.cloned.1.call-start = ((), (), s32[]{:S(2)}) async-start(), calls=%async_computation.9 | async-start | bytes 1310720 | tf_op jit(solution)/shard_map/reduce_scatter | solution.py:49
  683.1 231.9 %all-reduce.11.cloned.1.call-start = ((), (), s32[]{:S(2)}) async-start(), calls=%async_computation.10 | async-start | bytes 2097152 | tf_op jit(solution)/shard_map/psum | solution.py:22
  711.6 7.4 collective-permute-start.9
  711.6 7.4 collective-permute-start.11
  719.0 6.7 collective-permute-start.10
  729.1 223.7 %reduce-scatter.11.cloned.1.call-start = ((), (), s32[]{:S(2)}) async-start(), calls=%async_computation.11 | async-start | bytes 2621440 | tf_op jit(solution)/shard_map/reduce_scatter | solution.py:59
  919.9 32.9 %copy-start.2 = (f32[128,1024]{1,0:T(8,128)S(1)}, f32[128,1024]{1,0:T(8,128)}, u32[]{:S(2)}) copy-start(f32[128,1024]{1,0:T(8,128)} %param.5) | copy-start | bytes 1572868
  919.9 34.0 %copy-start.4 = (f32[128,512]{1,0:T(8,128)S(1)}, f32[128,512]{1,0:T(8,128)}, u32[]{:S(2)}) copy-start(f32[128,512]{1,0:T(8,128)} %copy-done.3) | copy-start | bytes 786436
  954.1 0.8 copy-start.5
Sparse Core Ops, SparseCore 0:
  26.4 188.3 all-reduce.4
  219.0 22.6 reduce-scatter.4
  260.3 186.0 all-reduce.6
  450.8 22.6 reduce-scatter.6
  494.3 185.9 all-reduce.8
  683.2 25.1 reduce-scatter.8
  729.2 185.7 all-reduce.10
  920.0 32.6 reduce-scatter.10
